TPU v7x, 256 devices: a whole 4x4x8 slice. The times are simulated.
256 devices in a mesh: section: 16 (over z_lo, y, core), tensor: 16 (over x, z_hi).
Axes of the slice: x: 4, y: 4, z: 8 (z_hi: 4, z_lo: 2; z = z_hi * 2 + z_lo), core: 2. Of those that a mesh axis runs over, the one named last changes fastest.
Arguments:
- hidden: bfloat16 [16, 64, 8192], P('section'), may hold values from -14 to 14
- head: bfloat16 [8192, 65536], P('section', 'tensor'), may hold values from -0.25 to 0.25
- exit_loss_weight: float32 [16], P('section'), may hold values from 2 to 32
Outputs:
- grad_hidden: float32 [1024, 8192], P('tensor', 'section')
- grad_head: bfloat16 [8192, 65536], P('section', 'tensor')
All inputs are finite; a program needn't handle non-finite values.
Results may differ from a plain program's by a relative error of at most 0.011.
Values may be sent and summed in bfloat16 or wider, within the bound.
No kernel may reach another device: no remote copies, remote signals or barrier semaphores. Data moves between devices by JAX's collectives and lax.ppermute only.
A program may use at most 128 MiB of HBM per device.

v0:
```python
import jax
import jax.numpy as jnp
from jax import lax
from jax.sharding import PartitionSpec as P

scaling_divisor = 2.0


def from_root(value, axis, source):
    kept = jnp.where(lax.axis_index(axis) == source, value, 0).astype(value.dtype)
    return lax.psum(kept, axis)


def local(hidden, head, exit_loss_weight):
    departure_number = lax.axis_size("section")
    tok_count = hidden.shape[1]
    row_count = departure_number * tok_count
    local_cols = lax.all_to_all(hidden, "section", split_axis=2, concat_axis=0, tiled=True)
    flat_hidden = local_cols.reshape(row_count, local_cols.shape[2])
    own_logits = lax.psum_scatter(
        jnp.dot(flat_hidden, head, preferred_element_type=jnp.float32),
        "section",
        scatter_dimension=0,
        tiled=True,
    )
    mentor_score_matrix = from_root(own_logits, "section", departure_number - 1)
    mentor_distribution = mentor_score_matrix / scaling_divisor
    local_smax = jnp.max(own_logits, axis=1)
    local_tmax = jnp.max(mentor_distribution, axis=1)
    student_max, teacher_max = lax.pmax((local_smax, local_tmax), "tensor")
    student_sum, teacher_sum = lax.psum(
        (
            jnp.sum(jnp.exp(own_logits - student_max[:, None]), axis=1),
            jnp.sum(jnp.exp(mentor_distribution - teacher_max[:, None]), axis=1),
        ),
        "tensor",
    )
    student_norm = student_max + jnp.log(student_sum)
    teacher_norm = teacher_max + jnp.log(teacher_sum)
    log_student = own_logits - student_norm[:, None]
    log_teacher = mentor_distribution - teacher_norm[:, None]
    log_mixture = jnp.logaddexp(log_student, log_teacher) - jnp.log(2.0)
    midpoint_difference = 0.5 * (log_student - log_mixture)
    student = jnp.exp(log_student)
    average = lax.psum(jnp.sum(student * midpoint_difference, axis=1), "tensor")
    grad_logits = (exit_loss_weight[0] * student * (midpoint_difference - average[:, None])).astype(
        jnp.bfloat16
    )
    piece = lax.all_gather(grad_logits, "section", axis=0, tiled=True)
    head_grad = lax.dot_general(
        flat_hidden, piece, (((0,), (0,)), ((), ())), preferred_element_type=jnp.float32
    )
    row_grad = lax.dot_general(
        piece, head, (((1,), (1,)), ((), ())), preferred_element_type=jnp.float32
    )
    hidden_part = row_grad
    head_grad, hidden_part = (head_grad, hidden_part)
    grad_hidden = lax.psum_scatter(hidden_part, "tensor", scatter_dimension=0, tiled=True)
    return (grad_hidden, head_grad.astype(jnp.bfloat16))


def solution(mesh):
    placed = (P("section", None, None), P("section", "tensor"), P("section"))
    return jax.shard_map(
        local,
        mesh=mesh,
        in_specs=placed,
        out_specs=(P("tensor", "section"), P("section", "tensor")),
        check_vma=False,
    )
```

profile of v0, /device:TPU:8, one launch (start us, length us, event | category | flops | bytes accessed | tf_op | source)
XLA Modules:
  0.0 624.9 jit_solution(6586606897295019781)
XLA Ops:
  7.2 0.0 reduce-scatter.3.cloned.1.call-start
  7.2 9.2 %copy.9 = bf16[1,64,8192]{1,0,2:T(2,128)(2,1)} copy(bf16[1,64,8192]{2,1,0:T(8,128)(2,1)} %param.3) | data formatting | bytes 2097152 | tf_op args[0]
  16.4 0.5 broadcast.12
  16.9 45.2 %reduce = bf16[8192,64]{1,0:T(8,128)(2,1)S(1)} reduce(bf16[8192,1,64]{2,1,0:T(2,128)(2,1)} %bitcast.21, bf16[]{:T(256)} %broadcast.12), dimensions={1}, to_apply=%bitcast.11.reduce_sub_computation | reduce | bytes 2097154
  62.1 1.5 reshape.14
  63.6 19.1 %all_to_all.15 = bf16[16,2,16384]{2,1,0:T(2,128)(2,1)S(1)} all-to-all(bf16[16,2,16384]{2,1,0:T(2,128)(2,1)S(1)} %reshape.14), channel_id=1, replica_groups=mesh['section'=16,'tensor'=16] {'section'}, dimensions={0} | all-to-all | bytes 2097152 | tf_op jit(solution)/shard_map/all_to_all | solution.py:18
  82.7 7.0 %reshape.15 = bf16[8192,1,64]{2,1,0:T(2,128)(2,1)} reshape(bf16[16,2,16384]{2,1,0:T(2,128)(2,1)S(1)} %all_to_all.15) | data formatting | bytes 2097152
  89.7 8.2 %copy.10 = bf16[1,64,8192]{2,1,0:T(8,128)(2,1)S(1)} copy(bf16[1,64,8192]{1,0,2:T(2,128)(2,1)} %bitcast.22) | data formatting | bytes 2097152 | tf_op jit(solution)/shard_map/all_to_all | solution.py:18
  97.8 0.4 copy.13
  98.2 0.1 bitcast_bitcast_fusion
  98.3 0.6 copy.11
  98.9 1.2 copy-done.2
  100.0 8.1 %fusion.2 = f32[1024,4096]{1,0:T(8,128)} fusion(bf16[1024,512]{1,0:T(8,128)(2,1)S(1)} %bitcast.25, bf16[512,4096]{1,0:T(8,128)(2,1)S(1)} %copy-done.2), kind=kOutput, calls=%fused_computation.13 | convolution fusion | flops 4294967296 | bytes 22020096 | tf_op jit(solution)/shard_map/dot_general | solution.py:21
  108.1 0.0 all-reduce.4.cloned.1.call-start
  108.2 100.5 %reduce-scatter.3.cloned.1.call-done = f32[64,4096]{1,0:T(8,128)} async-done(((f32[1024,4096]{1,0:T(8,128)}), f32[64,4096]{1,0:T(8,128)}) %reduce-scatter.3.cloned.1.call-update) | async-done | bytes 1048592 | tf_op jit(solution)/shard_map/reduce_scatter | solution.py:20
  208.6 2.5 fusion.1
  211.1 0.0 all-reduce.4.cloned.1.call-update
  211.1 0.0 all-gather.2.cloned.1.call-start
  211.8 122.8 %all-reduce.4.cloned.1.call-done = f32[64,4096]{1,0:T(8,128)} async-done(((f32[64,4096]{1,0:T(8,128)}), f32[64,4096]{1,0:T(8,128)}) %all-reduce.4.cloned.1.call-update) | async-done | bytes 1048592 | tf_op jit(solution)/shard_map/psum | solution.py:11
  334.6 1.5 multiply_reduce_fusion.1
  336.1 45.0 %all-reduce.1 = (f32[64]{0:T(128)S(1)}, f32[64]{0:T(128)S(1)}) all-reduce(f32[64]{0:T(128)S(1)} %multiply_reduce_fusion.1, f32[64]{0:T(128)S(1)} %get-tuple-element.14), channel_id=1, replica_groups=mesh['section'=16,'tensor'=16] {'tensor'}, use_global_device_ids=true, to_apply=%region_7.8 | all-reduce | flops 128 | bytes 1024 | tf_op jit(solution)/shard_map/pmax | solution.py:30
  381.1 1.7 exponential_reduce_fusion
  382.8 39.2 %all-reduce = (f32[64]{0:T(128)S(1)}, f32[64]{0:T(128)S(1)}) all-reduce(f32[64]{0:T(128)S(1)} %get-tuple-element.16, f32[64]{0:T(128)S(1)} %get-tuple-element.17), channel_id=1, replica_groups=mesh['section'=16,'tensor'=16] {'tensor'}, use_global_device_ids=true, to_apply=%region_9.10 | all-reduce | flops 128 | bytes 1024 | tf_op jit(solution)/shard_map/psum | solution.py:31
  422.1 2.4 multiply_reduce_fusion
  424.4 42.0 %psum.31 = f32[64]{0:T(128)S(1)} all-reduce(f32[64]{0:T(128)S(1)} %multiply_reduce_fusion), channel_id=1, replica_groups=mesh['section'=16,'tensor'=16] {'tensor'}, use_global_device_ids=true, to_apply=%region_11.12 | all-reduce | flops 64 | bytes 512 | tf_op jit(solution)/shard_map/psum | solution.py:45
  466.4 1.9 multiply_convert_fusion
  468.3 0.0 reduce-scatter.5.cloned.1.call-start
  468.4 49.5 %all-gather.2.cloned.1.call-done = bf16[1024,4096]{1,0:T(8,128)(2,1)} async-done(((bf16[64,4096]{1,0:T(8,128)(2,1)}), bf16[1024,4096]{1,0:T(8,128)(2,1)}) %all-gather.2.cloned.1.call-update) | async-done | bytes 8388624 | tf_op jit(solution)/shard_map/all_gather | solution.py:49
  517.9 10.5 %fusion.3 = f32[1024,512]{1,0:T(8,128)} fusion(bf16[1024,4096]{1,0:T(8,128)(2,1)} %all-gather.2.cloned.1.call-done, bf16[512,4096]{1,0:T(8,128)(2,1)} %param.4), kind=kOutput, calls=%fused_computation.14 | convolution fusion | flops 4294967296 | bytes 14680064 | tf_op jit(solution)/shard_map/dot_general | solution.py:53
  528.4 9.8 %fusion = bf16[512,4096]{0,1:T(8,128)(2,1)} fusion(bf16[1024,4096]{1,0:T(8,128)(2,1)} %all-gather.2.cloned.1.call-done, bf16[1024,512]{1,0:T(8,128)(2,1)S(1)} %bitcast.26), kind=kOutput, calls=%fused_computation.1 | convolution fusion | flops 4297064448 | bytes 13631488 | tf_op jit(solution)/shard_map/dot_general | solution.py:50
  538.1 6.3 %copy.12 = bf16[512,4096]{1,0:T(8,128)(2,1)} copy(bf16[512,4096]{0,1:T(8,128)(2,1)} %fusion) | data formatting | bytes 8388608
  544.4 73.9 %reduce-scatter.5.cloned.1.call-done = f32[64,512]{1,0:T(8,128)} async-done(((f32[1024,512]{1,0:T(8,128)}), f32[64,512]{1,0:T(8,128)}) %reduce-scatter.5.cloned.1.call-update) | async-done | bytes 131088 | tf_op jit(solution)/shard_map/reduce_scatter | solution.py:58
  (10 shorter events, 0.1 us)
Async XLA Ops:
  7.2 201.4 %reduce-scatter.3.cloned.1.call-start = ((), (), s32[]{:S(2)}) async-start(), calls=%async_computation.3 | async-start | bytes 17825792 | tf_op jit(solution)/shard_map/reduce_scatter | solution.py:20
  97.8 2.2 copy-start.2
  108.1 226.5 %all-reduce.4.cloned.1.call-start = ((), (), s32[]{:S(2)}) async-start(), calls=%async_computation.4 | async-start | bytes 2097152 | tf_op jit(solution)/shard_map/psum | solution.py:11
  208.6 172.5 %copy-start.1 = (f32[64,4096]{1,0:T(8,128)S(1)}, f32[64,4096]{1,0:T(8,128)}, u32[]{:S(2)}) copy-start(f32[64,4096]{1,0:T(8,128)} %reduce-scatter.3.cloned.1.call-done) | copy-start | bytes 3145732
  211.1 306.8 %all-gather.2.cloned.1.call-start = ((), (), s32[]{:S(2)}) async-start(), calls=%async_computation.5 | async-start | bytes 8912896 | tf_op jit(solution)/shard_map/all_gather | solution.py:49
  334.6 131.8 %copy-start = (f32[64,4096]{1,0:T(8,128)S(1)}, f32[64,4096]{1,0:T(8,128)}, u32[]{:S(2)}) copy-start(f32[64,4096]{1,0:T(8,128)} %all-reduce.4.cloned.1.call-done) | copy-start | bytes 3145732
  468.3 150.0 %reduce-scatter.5.cloned.1.call-start = ((), (), s32[]{:S(2)}) async-start(), calls=%async_computation.6 | async-start | bytes 2228224 | tf_op jit(solution)/shard_map/reduce_scatter | solution.py:58
Sparse Core Ops, SparseCore 0:
  108.2 100.3 reduce-scatter.2
  211.8 122.7 all-reduce.3
  468.5 49.3 all-gather.1
  528.5 89.8 reduce-scatter.4
where the time goes:
time: 626 us; the launch traced here: 625 us
  waiting for transfers between devices  347 us (55%)
  blocking collectives  145 us (23%)
  other arithmetic  55.1 us (9%)
  local copies, waits for them, and re-layouts  34.7 us (6%)
  matrix products  28.3 us (5%)
  between operations  14.5 us (2%)
    psum x1, waiting for transfers between devices, from_root(): return lax.psum(kept, axis)  123 us
    reduce_scatter x1, waiting for transfers between devices, local(): lax.psum_scatter(jnp.dot(flat_hidden, head, preferred_element_type=jnp.fl...  100 us
    reduce_scatter x1, waiting for transfers between devices, local(): lax.psum_scatter(hidden_part, 'tensor', scatter_dimension=0, tiled=True)  73.9 us
    all_gather x1, waiting for transfers between devices, local(): piece = lax.all_gather(grad_logits, 'section', axis=0, tiled=True)  49.5 us
    unnamed x1, other arithmetic  45.2 us
    pmax x1, blocking collectives, local(): student_max, teacher_max = lax.pmax((local_smax, local_tmax), 'tensor')  45 us
    psum x1, blocking collectives, local(): average = lax.psum(jnp.sum(student * midpoint_difference, axis=1), 'tensor')  42 us
    psum x1, blocking collectives, local(): lax.psum((jnp.sum(jnp.exp(own_logits - student_max[:, None]), axis=1), jn...  39.2 us
  transfers between devices with their start and end apart: 4, of which 4 were waited for; matrix products, arithmetic and copies ran while one was open for 3% of the time, Pallas kernels for 0%

commit v1 on v0

--- a/solution.py
+++ b/solution.py
@@ -15,7 +15,12 @@
     departure_number = lax.axis_size("section")
     tok_count = hidden.shape[1]
     row_count = departure_number * tok_count
-    local_cols = lax.all_to_all(hidden, "section", split_axis=2, concat_axis=0, tiled=True)
+    local_cols = jnp.concatenate(
+        lax.all_to_all(
+            jnp.stack(jnp.split(hidden, lax.axis_size("section"), axis=2), axis=0), "section", 0, 0
+        ),
+        axis=0,
+    )
     flat_hidden = local_cols.reshape(row_count, local_cols.shape[2])
     own_logits = lax.psum_scatter(
         jnp.dot(flat_hidden, head, preferred_element_type=jnp.float32),

time: 626 us -> 566 us (0.904)
  other arithmetic: 55.1 us -> 9.88 us
  local copies, waits for them, and re-layouts: 34.7 us -> 13.9 us
    unnamed x1 -> x0, other arithmetic: 45.2 us -> none
    unnamed x12 -> x21, local copies, waits for them, and re-layouts: 25.9 us -> 13.1 us
    all_to_all x3 -> x0, local copies, waits for them, and re-layouts: 8.81 us -> none  [local(): lax.all_to_all(hidden, 'section', split_axis=2, concat_axis=0, tiled=True)]
    reduce_scatter x1, waiting for transfers between devices: 73.9 us -> 80.3 us  [local(): lax.psum_scatter(hidden_part, 'tensor', scatter_dimension=0, tiled=True)]
  transfers between devices with their start and end apart: 4 -> 4, of which waited for: 4 -> 4; matrix products, arithmetic and copies ran while one was open for 3% -> 2% of each run, Pallas kernels for 0% -> 0%
where the time goes in v1:
time: 566 us; the launch traced here: 565 us
  waiting for transfers between devices  353 us (62%)
  blocking collectives  145 us (26%)
  matrix products  28 us (5%)
  between operations  14.5 us (3%)
  local copies, waits for them, and re-layouts  13.9 us (2%)
  other arithmetic  9.88 us (2%)
    psum x1, waiting for transfers between devices, from_root(): return lax.psum(kept, axis)  123 us
    reduce_scatter x1, waiting for transfers between devices, local(): lax.psum_scatter(jnp.dot(flat_hidden, head, preferred_element_type=jnp.fl...  100 us
    reduce_scatter x1, waiting for transfers between devices, local(): lax.psum_scatter(hidden_part, 'tensor', scatter_dimension=0, tiled=True)  80.3 us
    all_gather x1, waiting for transfers between devices, local(): piece = lax.all_gather(grad_logits, 'section', axis=0, tiled=True)  49.5 us
    pmax x1, blocking collectives, local(): student_max, teacher_max = lax.pmax((local_smax, local_tmax), 'tensor')  45 us
    psum x1, blocking collectives, local(): average = lax.psum(jnp.sum(student * midpoint_difference, axis=1), 'tensor')  42 us
    psum x1, blocking collectives, local(): lax.psum((jnp.sum(jnp.exp(own_logits - student_max[:, None]), axis=1), jn...  39.1 us
    all_to_all x1, blocking collectives, local(): lax.all_to_all(jnp.stack(jnp.split(hidden, lax.axis_size('section'), axis...  19.1 us
  transfers between devices with their start and end apart: 4, of which 4 were waited for; matrix products, arithmetic and copies ran while one was open for 2% of the time, Pallas kernels for 0%

profile of v1, /device:TPU:8, one launch (start us, length us, event | category | flops | bytes accessed | tf_op | source)
XLA Modules:
  0.0 564.8 jit_solution(17445542676295770635)
XLA Ops:
  7.2 1.0 bitcast_dynamic-update-slice_fusion.15
  8.2 1.1 bitcast_dynamic-update-slice_fusion.14
  9.3 0.8 bitcast_dynamic-update-slice_fusion.13
  10.2 0.8 bitcast_dynamic-update-slice_fusion.12
  11.0 0.8 bitcast_dynamic-update-slice_fusion.11
  11.8 0.8 bitcast_dynamic-update-slice_fusion.10
  12.7 0.8 bitcast_dynamic-update-slice_fusion.9
  13.5 0.8 bitcast_dynamic-update-slice_fusion.8
  14.4 0.8 bitcast_dynamic-update-slice_fusion.7
  15.2 0.8 bitcast_dynamic-update-slice_fusion.6
  16.1 0.8 bitcast_dynamic-update-slice_fusion.5
  16.9 0.8 bitcast_dynamic-update-slice_fusion.4
  17.8 0.8 bitcast_dynamic-update-slice_fusion.3
  18.6 0.8 bitcast_dynamic-update-slice_fusion.2
  19.4 0.8 bitcast_dynamic-update-slice_fusion.1
  20.3 0.8 bitcast_dynamic-update-slice_fusion
  21.1 19.1 %all_to_all.5 = bf16[16,1,64,512]{3,2,1,0:T(8,128)(2,1)S(1)} all-to-all(bf16[16,1,64,512]{3,2,1,0:T(8,128)(2,1)S(1)} %bitcast_dynamic-update-slice_fusion), channel_id=1, replica_groups=mesh['section'=16,'tensor'=16] {'section'}, dimensions={0} | all-to-all | bytes 2097152 | tf_op jit(solution)/shard_map/all_to_all | solution.py:19
  40.3 8.1 %fusion.1 = f32[1024,4096]{1,0:T(8,128)} fusion(bf16[1024,512]{1,0:T(8,128)(2,1)S(1)} %bitcast.41, bf16[512,4096]{1,0:T(8,128)(2,1)S(1)} %copy-done.2), kind=kOutput, calls=%fused_computation.27 | convolution fusion | flops 4294967296 | bytes 22020096 | tf_op jit(solution)/shard_map/dot_general | solution.py:26
  48.4 100.5 %reduce-scatter.3.cloned.1.call-done = f32[64,4096]{1,0:T(8,128)} async-done(((f32[1024,4096]{1,0:T(8,128)}), f32[64,4096]{1,0:T(8,128)}) %reduce-scatter.3.cloned.1.call-update) | async-done | bytes 1048592 | tf_op jit(solution)/shard_map/reduce_scatter | solution.py:25
  148.9 2.5 fusion
  152.0 122.8 %all-reduce.4.cloned.1.call-done = f32[64,4096]{1,0:T(8,128)} async-done(((f32[64,4096]{1,0:T(8,128)}), f32[64,4096]{1,0:T(8,128)}) %all-reduce.4.cloned.1.call-update) | async-done | bytes 1048592 | tf_op jit(solution)/shard_map/psum | solution.py:11
  274.8 1.5 multiply_reduce_fusion.1
  276.3 45.0 %all-reduce.1 = (f32[64]{0:T(128)S(1)}, f32[64]{0:T(128)S(1)}) all-reduce(f32[64]{0:T(128)S(1)} %multiply_reduce_fusion.1, f32[64]{0:T(128)S(1)} %get-tuple-element.6), channel_id=1, replica_groups=mesh['section'=16,'tensor'=16] {'tensor'}, use_global_device_ids=true, to_apply=%region_7.8 | all-reduce | flops 128 | bytes 1024 | tf_op jit(solution)/shard_map/pmax | solution.py:35
  321.4 1.7 exponential_reduce_fusion
  323.1 39.1 %all-reduce = (f32[64]{0:T(128)S(1)}, f32[64]{0:T(128)S(1)}) all-reduce(f32[64]{0:T(128)S(1)} %get-tuple-element.8, f32[64]{0:T(128)S(1)} %get-tuple-element.9), channel_id=1, replica_groups=mesh['section'=16,'tensor'=16] {'tensor'}, use_global_device_ids=true, to_apply=%region_9.10 | all-reduce | flops 128 | bytes 1024 | tf_op jit(solution)/shard_map/psum | solution.py:36
  362.1 2.4 multiply_reduce_fusion
  364.5 42.0 %psum.31 = f32[64]{0:T(128)S(1)} all-reduce(f32[64]{0:T(128)S(1)} %multiply_reduce_fusion), channel_id=1, replica_groups=mesh['section'=16,'tensor'=16] {'tensor'}, use_global_device_ids=true, to_apply=%region_11.12 | all-reduce | flops 64 | bytes 512 | tf_op jit(solution)/shard_map/psum | solution.py:50
  406.5 1.9 multiply_convert_fusion
  408.4 49.5 %all-gather.2.cloned.1.call-done = bf16[1024,4096]{1,0:T(8,128)(2,1)} async-done(((bf16[64,4096]{1,0:T(8,128)(2,1)}), bf16[1024,4096]{1,0:T(8,128)(2,1)}) %all-gather.2.cloned.1.call-update) | async-done | bytes 8388624 | tf_op jit(solution)/shard_map/all_gather | solution.py:54
  457.9 10.5 %fusion.2 = f32[1024,512]{1,0:T(8,128)} fusion(bf16[1024,4096]{1,0:T(8,128)(2,1)} %all-gather.2.cloned.1.call-done, bf16[512,4096]{1,0:T(8,128)(2,1)} %param.4), kind=kOutput, calls=%fused_computation.28 | convolution fusion | flops 4294967296 | bytes 14680064 | tf_op jit(solution)/shard_map/dot_general | solution.py:58
  468.4 9.5 %convolution_convert_fusion = bf16[512,4096]{1,0:T(8,128)(2,1)} fusion(bf16[1024,512]{1,0:T(8,128)(2,1)S(1)} %bitcast.42, bf16[1024,4096]{1,0:T(8,128)(2,1)} %all-gather.2.cloned.1.call-done), kind=kOutput, calls=%fused_computation | convolution fusion | flops 4297064448 | bytes 13631488 | tf_op jit(solution)/shard_map/dot_general | solution.py:55
  478.0 80.3 %reduce-scatter.5.cloned.1.call-done = f32[64,512]{1,0:T(8,128)} async-done(((f32[1024,512]{1,0:T(8,128)}), f32[64,512]{1,0:T(8,128)}) %reduce-scatter.5.cloned.1.call-update) | async-done | bytes 131088 | tf_op jit(solution)/shard_map/reduce_scatter | solution.py:63
  (16 shorter events, 0.3 us)
Async XLA Ops:
  7.2 141.7 %reduce-scatter.3.cloned.1.call-start = ((), (), s32[]{:S(2)}) async-start(), calls=%async_computation.3 | async-start | bytes 17825792 | tf_op jit(solution)/shard_map/reduce_scatter | solution.py:25
  7.2 33.0 %copy-start.2 = (bf16[512,4096]{1,0:T(8,128)(2,1)S(1)}, bf16[512,4096]{1,0:T(8,128)(2,1)}, u32[]{:S(2)}) copy-start(bf16[512,4096]{1,0:T(8,128)(2,1)} %param.4) | copy-start | bytes 12582916
  48.3 226.5 %all-reduce.4.cloned.1.call-start = ((), (), s32[]{:S(2)}) async-start(), calls=%async_computation.4 | async-start | bytes 2097152 | tf_op jit(solution)/shard_map/psum | solution.py:11
  148.9 172.5 %copy-start.1 = (f32[64,4096]{1,0:T(8,128)S(1)}, f32[64,4096]{1,0:T(8,128)}, u32[]{:S(2)}) copy-start(f32[64,4096]{1,0:T(8,128)} %reduce-scatter.3.cloned.1.call-done) | copy-start | bytes 3145732
  151.3 306.6 %all-gather.2.cloned.1.call-start = ((), (), s32[]{:S(2)}) async-start(), calls=%async_computation.5 | async-start | bytes 8912896 | tf_op jit(solution)/shard_map/all_gather | solution.py:54
  274.8 131.7 %copy-start = (f32[64,4096]{1,0:T(8,128)S(1)}, f32[64,4096]{1,0:T(8,128)}, u32[]{:S(2)}) copy-start(f32[64,4096]{1,0:T(8,128)} %all-reduce.4.cloned.1.call-done) | copy-start | bytes 3145732
  408.4 149.9 %reduce-scatter.5.cloned.1.call-start = ((), (), s32[]{:S(2)}) async-start(), calls=%async_computation.6 | async-start | bytes 2228224 | tf_op jit(solution)/shard_map/reduce_scatter | solution.py:63
Sparse Core Ops, SparseCore 0:
  48.5 100.3 reduce-scatter.2
  152.1 122.7 all-reduce.3
  408.5 49.3 all-gather.1
  468.6 89.6 reduce-scatter.4
